TPU v7x, 256 devices: a whole 4x4x8 slice. The times are simulated.
256 devices in a mesh: seq: 16 (over y, x), fsdp: 16 (over z, core).
Axes of the slice: x: 4, y: 4, z: 8, core: 2. Of those that a mesh axis runs over, the one named last changes fastest.
Arguments:
- byte_rows: bfloat16 [16, 16384, 512], P('fsdp', 'seq'), may hold values from -6 to 6
- cotangent: bfloat16 [16, 16384, 512], P('fsdp', 'seq'), may hold values from -6 to 6
- doc_ids: int32 [16, 16384], P('fsdp', 'seq'), may hold values from 0 to 31, never falling along the last dimension, each value on 1 to 2048 neighbouring positions
- conv_weight: bfloat16 [8, 32, 16, 16], replicated, may hold values from -0.5 to 0.5
- norm_gain: float32 [512], replicated, may hold values from 0.5 to 1.5
- proj_weight: bfloat16 [4096, 512], P('fsdp'), may hold values from -0.25 to 0.25
- round_seed: int32 [1], replicated, may hold values from 0 to 1073741823
- step_count: int32 [1], replicated, may hold values from 0 to 999999
Outputs:
- grad_bytes: float32 [16, 16384, 512], P('fsdp', 'seq')
- grad_proj: float32 [4096, 512], P('fsdp')
- grad_conv: float32 [8, 32, 16, 16], replicated
- grad_gain: float32 [512], replicated
Inputs may be any that keep to these rules, and one draw needn't show every extreme that they name: `doc_ids`: along each sequence the document numbers never fall; no document covers more than 2048 bytes, and one covers exactly 2048.
All inputs are finite; a program needn't handle non-finite values.
Results may differ from a plain program's by a relative error of at most 0.0046.
Values may be sent and summed in bfloat16 or wider, within the bound.
No kernel may reach another device: no remote copies, remote signals or barrier semaphores. Data moves between devices by JAX's collectives and lax.ppermute only.
A program may use at most 128 MiB of HBM per device.

v0:
```python
import math
import jax
import jax.numpy as jnp
from jax import lax
from jax.sharding import PartitionSpec as P

GROUPS = 32
KERNEL = 8
STRIDE = 4
CG = 16
GELU_A = 0.7978845608028654
GELU_B = 0.044715
QUANT = 0.25


def shifted(value, axis, steps):
    count = lax.axis_size(axis)
    initial, last = (max(0, -steps), min(count, count - steps))
    return lax.ppermute(value, axis, [(source, source + steps) for source in range(initial, last)])


def gelu_grad(values):
    tangent = jnp.tanh(GELU_A * (values + GELU_B * values * values * values))
    return 0.5 * (1.0 + tangent) + 0.5 * values * (1.0 - tangent * tangent) * GELU_A * (
        1.0 + 3.0 * GELU_B * values * values
    )


def mix_bits(flat_index, seed_value, step_value):
    hashed = (
        flat_index * jnp.int32(-1640531535)
        + seed_value * jnp.int32(-2048144777)
        + step_value * jnp.int32(-1028477379)
    )
    hashed = hashed ^ lax.shift_right_logical(hashed, jnp.int32(16))
    hashed = hashed * jnp.int32(2146121005)
    hashed = hashed ^ lax.shift_right_logical(hashed, jnp.int32(15))
    hashed = hashed * jnp.int32(-2073254261)
    hashed = hashed ^ lax.shift_right_logical(hashed, jnp.int32(16))
    return lax.shift_right_logical(hashed, jnp.int32(8)).astype(jnp.float32) / 16777216.0


def split_bf16(value):
    high = value.astype(jnp.bfloat16)
    low = (value - high.astype(jnp.float32)).astype(jnp.bfloat16)
    return (high, low)


def dot_f32(lhs, rhs, dims):
    return lax.dot_general(lhs, rhs, (dims, ((), ())), preferred_element_type=jnp.float32)


def per_device(
    byte_rows, cotangent, doc_ids, conv_weight, norm_gain, proj_weight, round_seed, step_count
):
    byte_block = byte_rows[0]
    upstream = cotangent[0]
    doc_block = doc_ids[0]
    length = byte_block.shape[0]
    row_width = byte_block.shape[1]
    patches = length // STRIDE
    half = STRIDE * row_width
    panel_rows = proj_weight.shape[0]
    next_bytes, next_up, next_docs = shifted(
        (byte_block[:STRIDE], upstream[:STRIDE], doc_block[:STRIDE]), "seq", -1
    )
    bytes_lo = byte_block.reshape(patches, half)
    bytes_hi = jnp.concatenate([bytes_lo[1:], next_bytes.reshape(1, half)], 0)
    up_lo = upstream.reshape(patches, half)
    up_hi = jnp.concatenate([up_lo[1:], next_up.reshape(1, half)], 0)
    docs_lo = doc_block.reshape(patches, STRIDE)
    docs_hi = jnp.concatenate([docs_lo[1:], next_docs.reshape(1, STRIDE)], 0)
    is_last = lax.axis_index("seq") == lax.axis_size("seq") - 1
    patch_ids = lax.broadcasted_iota(jnp.int32, (patches, STRIDE), 0)
    spilled = is_last & (patch_ids == patches - 1)
    keep_lo = docs_lo == docs_lo[:, :1]
    keep_hi = (docs_hi == docs_lo[:, :1]) & jnp.logical_not(spilled)

    def spread(keep):
        return jnp.broadcast_to(keep[:, :, None], (patches, STRIDE, row_width)).reshape(
            patches, half
        )

    keep_lo_f = spread(keep_lo.astype(jnp.float32))
    keep_hi_f = spread(keep_hi.astype(jnp.float32))
    win_lo = bytes_lo * keep_lo_f.astype(jnp.bfloat16)
    win_hi = bytes_hi * keep_hi_f.astype(jnp.bfloat16)
    group_eye = jnp.eye(GROUPS, dtype=jnp.bfloat16)
    dense_weight = (conv_weight[:, :, :, None, :] * group_eye[None, :, None, :, None]).reshape(
        KERNEL, row_width, row_width
    )
    weight_lo = dense_weight[:STRIDE].reshape(half, row_width)
    weight_hi = dense_weight[STRIDE:].reshape(half, row_width)
    hidden = dot_f32(win_lo, weight_lo, ((1,), (0,))) + dot_f32(win_hi, weight_hi, ((1,), (0,)))
    factor = lax.rsqrt(jnp.mean(hidden * hidden, axis=-1, keepdims=True) + 1e-06)
    normed = (hidden * factor * norm_gain).astype(jnp.bfloat16)
    full_proj = lax.all_gather(proj_weight, "fsdp", axis=0, tiled=True)
    proj_lo = full_proj[:half]
    proj_hi = full_proj[half:]
    pre_lo = dot_f32(normed, proj_lo, ((1,), (1,)))
    pre_hi = dot_f32(normed, proj_hi, ((1,), (1,)))
    grad_pre_lo = (up_lo.astype(jnp.float32) * keep_lo_f * gelu_grad(pre_lo)).astype(jnp.bfloat16)
    grad_pre_hi = (up_hi.astype(jnp.float32) * keep_hi_f * gelu_grad(pre_hi)).astype(jnp.bfloat16)
    proj_part = jnp.concatenate(
        [dot_f32(grad_pre_lo, normed, ((0,), (0,))), dot_f32(grad_pre_hi, normed, ((0,), (0,)))], 0
    )
    panel_part = lax.psum_scatter(proj_part, "fsdp", scatter_dimension=0, tiled=True)
    grad_norm = dot_f32(grad_pre_lo, proj_lo, ((1,), (0,))) + dot_f32(
        grad_pre_hi, proj_hi, ((1,), (0,))
    )
    gain_part = jnp.sum(grad_norm * hidden * factor, axis=0)
    gained = norm_gain * grad_norm
    grad_hidden = factor * gained - hidden * factor * factor * factor * jnp.mean(
        gained * hidden, axis=-1, keepdims=True
    )
    gh_high, gh_low = split_bf16(grad_hidden)

    def window_grad(window):
        full = dot_f32(window, gh_high, ((0,), (0,))) + dot_f32(window, gh_low, ((0,), (0,)))
        blocks = full.reshape(STRIDE, GROUPS, CG, GROUPS, CG)
        mask = jnp.eye(GROUPS, dtype=jnp.float32)[None, :, None, :, None]
        return jnp.sum(blocks * mask, axis=3)

    conv_part = jnp.concatenate([window_grad(win_lo), window_grad(win_hi)], 0)

    def back_taps(weight, keep_f):
        taps = dot_f32(gh_high, weight, ((1,), (1,))) + dot_f32(gh_low, weight, ((1,), (1,)))
        return (taps * keep_f).reshape(length, row_width)

    back_lower = back_taps(weight_lo, keep_lo_f)
    back_upper = back_taps(weight_hi, keep_hi_f)
    incoming = shifted(back_upper[length - STRIDE :], "seq", 1)
    back_rows = back_lower + jnp.concatenate([incoming, back_upper[: length - STRIDE]], 0)
    grad_bytes = (upstream.astype(jnp.float32) + back_rows)[None]
    conv_size = conv_part.size
    small = jnp.concatenate([conv_part.reshape(-1), gain_part]).reshape(-1, row_width)
    small = lax.psum(small, "fsdp")
    joined = lax.psum(jnp.concatenate([panel_part, small], 0), "seq")
    proj_sum = joined[:panel_rows]
    small_sum = joined[panel_rows:].reshape(-1)
    conv_sum = small_sum[:conv_size].reshape(conv_part.shape)
    gain_sum = small_sum[conv_size:]
    total_patches = patches * lax.axis_size("seq") * lax.axis_size("fsdp")
    grad_scale = 1.0 / math.sqrt(total_patches)
    first_panel = lax.axis_index("fsdp") * jnp.int32(panel_rows)
    row_index = first_panel + jnp.arange(panel_rows, dtype=jnp.int32)
    flat_index = (
        row_index[:, None] * jnp.int32(row_width) + jnp.arange(row_width, dtype=jnp.int32)[None, :]
    )
    dither_noise = mix_bits(flat_index, round_seed[0], step_count[0])
    grad_proj = proj_sum * grad_scale + QUANT * (dither_noise - 0.5)
    return (grad_bytes, grad_proj, conv_sum * grad_scale, gain_sum * grad_scale)


def solution(mesh):
    in_specs = (
        P("fsdp", "seq", None),
        P("fsdp", "seq", None),
        P("fsdp", "seq"),
        P(),
        P(),
        P("fsdp", None),
        P(),
        P(),
    )
    out_specs = (P("fsdp", "seq", None), P("fsdp", None), P(), P())
    return jax.shard_map(
        per_device, mesh=mesh, in_specs=in_specs, out_specs=out_specs, check_vma=False
    )
```

profile of v0, /device:TPU:32, one launch (start us, length us, event | category | flops | bytes accessed | tf_op | source)
XLA Modules:
  0.0 527.3 jit_solution(15065183540422117678)
XLA Ops:
  8.0 1.3 collective-permute-start.1
  10.0 1.3 collective-permute-start
  11.9 1.3 collective-permute-start.2
  13.8 1.3 reduce.13
  16.3 1.5 slice.78
  17.8 1.2 slice.86
  19.0 1.6 reshape.263
  20.6 1.4 reshape_squeeze.11
  22.0 1.5 concatenate.56
  23.5 1.7 slice.94
  25.9 1.5 mul.283
  28.2 11.2 %broadcast_multiply_fusion = bf16[8,32,16,32,16]{4,3,2,1,0:T(8,128)(2,1)} fusion(bf16[32,32]{1,0:T(8,128)(2,1)S(1)} %fusion.39, bf16[8,32,16,16]{3,2,1,0:T(8,128)(2,1)S(1)} %copy.23), kind=kLoop, calls=%fused_computation.2 | loop fusion | flops 2097152 | bytes 4327424 | tf_op jit(solution)/shard_map/mul | solution.py:89
  39.4 25.7 %fusion.44 = (bf16[4,32,16,32,16]{4,3,2,1,0:T(8,128)(2,1)}, bf16[4,32,16,32,16]{4,3,2,1,0:T(8,128)(2,1)}) fusion(bf16[8,32,16,32,16]{4,3,2,1,0:T(8,128)(2,1)} %broadcast_multiply_fusion), kind=kLoop, calls=%fused_computation.87 | loop fusion | bytes 8388608 | tf_op jit(solution)/shard_map/slice | solution.py:93
  65.1 28.7 %reshape.252 = bf16[2048,512]{1,0:T(8,128)(2,1)} reshape(bf16[4,32,16,32,16]{4,3,2,1,0:T(8,128)(2,1)} %get-tuple-element.29) | data formatting | bytes 4194304 | tf_op jit(solution)/shard_map/reshape | solution.py:92
  93.8 28.2 %reshape.253 = bf16[2048,512]{1,0:T(8,128)(2,1)S(1)} reshape(bf16[4,32,16,32,16]{4,3,2,1,0:T(8,128)(2,1)} %get-tuple-element.28) | data formatting | bytes 4194304 | tf_op jit(solution)/shard_map/reshape | solution.py:93
  122.0 1.6 slice.87
  123.6 2.6 fusion.45
  126.9 2.2 copy.32
  134.1 4.3 fusion.15
  138.5 2.9 fusion.49
  141.8 1.6 copy-done.22
  143.4 1.8 fusion.8
  145.2 2.7 fusion.48
  150.1 1.1 copy-done.7
  151.2 1.0 fusion.40
  152.2 2.8 convolution_add_fusion.1
  155.1 19.8 %reshape.258 = f32[4,32,16,32,16]{4,3,2,1,0:T(8,128)} reshape(f32[2048,512]{1,0:T(8,128)} %convolution_add_fusion.1) | data formatting | bytes 8388608 | tf_op jit(solution)/shard_map/reshape | solution.py:120
  174.9 1.7 fusion.50
  176.6 2.8 convolution_add_fusion
  179.4 19.8 %reshape.260 = f32[4,32,16,32,16]{4,3,2,1,0:T(8,128)} reshape(f32[2048,512]{1,0:T(8,128)} %convolution_add_fusion) | data formatting | bytes 8388608 | tf_op jit(solution)/shard_map/reshape | solution.py:120
  199.2 25.5 %multiply_reduce_fusion.1 = (f32[4,32,16,16]{3,2,1,0:T(8,128)S(1)}, f32[4,32,16,16]{3,2,1,0:T(8,128)}) fusion(f32[4,32,16,32,16]{4,3,2,1,0:T(8,128)} %reshape.258, f32[32,32]{1,0:T(8,128)S(1)} %fusion.38, f32[4,32,16,32,16]{4,3,2,1,0:T(8,128)} %reshape.260), kind=kLoop, calls=%fused_computation.1 | loop fusion | flops 4128768 | bytes 8654848 | tf_op jit(solution)/shard_map/reduce_sum | solution.py:122
  224.7 2.7 pad_maximum_fusion.1
  227.5 2.2 reshape.261
  230.5 7.7 %pad_maximum_fusion = f32[4096,512]{1,0:T(8,128)} fusion(f32[2048,512]{1,0:T(8,128)} %fusion.49, f32[2048,512]{1,0:T(8,128)} %fusion.48), kind=kLoop, calls=%fused_computation.3 | loop fusion | flops 2097152 | bytes 16777216 | tf_op jit(solution)/shard_map/concatenate | solution.py:104
  242.0 1.4 copy-done.8
  243.4 5.8 %collective-permute-start.3 = (f32[4,512]{1,0:T(4,128)S(1)}, f32[4,512]{1,0:T(4,128)S(1)}, u32[]{:S(2)}, u32[]{:S(2)}) collective-permute-start(f32[4,512]{1,0:T(4,128)S(1)} %slice.92), channel_id=1, source_target_pairs={{0,16},{16,32},{32,48},{48,64},{64,80},{80,96},{96,112},{112,128},... | collective-permute-start | bytes 24584 | tf_op jit(solution)/shard_map/ppermute | solution.py:19
  249.2 3.7 fusion.46
  252.9 89.3 %all-reduce.3.cloned.1.call-done = f32[129,512]{1,0:T(8,128)} async-done(((f32[129,512]{1,0:T(8,128)}), f32[129,512]{1,0:T(8,128)}) %all-reduce.3.cloned.1.call-update) | async-done | bytes 264208 | tf_op jit(solution)/shard_map/psum | solution.py:137
  342.1 71.0 %reduce-scatter.2.cloned.1.call-done = f32[256,512]{1,0:T(8,128)} async-done(((f32[4096,512]{1,0:T(8,128)}), f32[256,512]{1,0:T(8,128)}) %reduce-scatter.2.cloned.1.call-update) | async-done | bytes 524304 | tf_op jit(solution)/shard_map/reduce_scatter | solution.py:107
  413.2 2.1 pad_maximum_fusion.2
  415.3 4.3 fusion.1
  419.6 3.0 reshape.257
  422.6 1.9 concatenate.64
  424.5 4.1 fusion.16
  428.6 86.9 %all-reduce.5.cloned.1.call-done = f32[385,512]{1,0:T(8,128)} async-done(((f32[385,512]{1,0:T(8,128)}), f32[385,512]{1,0:T(8,128)}) %all-reduce.5.cloned.1.call-update) | async-done | bytes 788496 | tf_op jit(solution)/shard_map/psum | solution.py:138
  515.5 1.0 slice_multiply_fusion.1
  517.2 1.8 copy.30
  519.6 1.2 fusion.37
  (103 shorter events, 18.0 us)
Async XLA Ops:
  7.2 10.6 %copy-start.5 = (bf16[1,1024,512]{2,1,0:T(8,128)(2,1)S(1)}, bf16[1,1024,512]{2,1,0:T(8,128)(2,1)}, u32[]{:S(2)}) copy-start(bf16[1,1024,512]{2,1,0:T(8,128)(2,1)} %param.9) | copy-start | bytes 3145732
  7.2 126.9 %all-gather.2.cloned.1.call-start = ((), (), s32[]{:S(2)}) async-start(), calls=%async_computation.1 | async-start | bytes 4456448 | tf_op jit(solution)/shard_map/all_gather | solution.py:97
  8.0 118.3 %collective-permute-start.1 = (s32[4]{0:T(128)S(1)}, s32[4]{0:T(128)S(1)}, u32[]{:S(2)}, u32[]{:S(2)}) collective-permute-start(s32[4]{0:T(128)S(1)} %slice_bitcast_fusion.2), channel_id=1, source_target_pairs={{16,0},{32,16},{48,32},{64,48},{80,64},{96,80},{112,96},{128,112},... | collective-permute-start | bytes 56 | tf_op jit(solution)/shard_map/ppermute | solution.py:19
  10.0 120.7 %collective-permute-start = (bf16[4,512]{1,0:T(4,128)(2,1)S(1)}, bf16[4,512]{1,0:T(4,128)(2,1)S(1)}, u32[]{:S(2)}, u32[]{:S(2)}) collective-permute-start(bf16[4,512]{1,0:T(4,128)(2,1)S(1)} %slice_bitcast_fusion.1), channel_id=1, source_target_pairs={{16,0},{32,16},{48,32},{64,48},{80,64},{96,80},{112,96},{128,112},... | collective-permute-start | bytes 12296 | tf_op jit(solution)/shard_map/ppermute | solution.py:19
  11.9 120.2 %collective-permute-start.2 = (bf16[4,512]{1,0:T(4,128)(2,1)S(1)}, bf16[4,512]{1,0:T(4,128)(2,1)S(1)}, u32[]{:S(2)}, u32[]{:S(2)}) collective-permute-start(bf16[4,512]{1,0:T(4,128)(2,1)S(1)} %slice_bitcast_fusion), channel_id=1, source_target_pairs={{16,0},{32,16},{48,32},{64,48},{80,64},{96,80},{112,96},{128,112},... | collective-permute-start | bytes 12296 | tf_op jit(solution)/shard_map/ppermute | solution.py:19
  13.3 328.9 %all-reduce.3.cloned.1.call-start = ((), (), s32[]{:S(2)}) async-start(), calls=%async_computation.3 | async-start | bytes 557056 | tf_op jit(solution)/shard_map/psum | solution.py:137
  19.0 1.6 copy-start.4
  22.0 3.6 copy-start.20
  25.7 1.7 copy-start.19
  93.8 28.2 %copy-start.14 = (bf16[1,1020,512]{2,1,0:T(8,128)(2,1)S(1)}, bf16[1,1020,512]{2,1,0:T(8,128)(2,1)}, u32[]{:S(2)}) copy-start(bf16[1,1020,512]{2,1,0:T(8,128)(2,1)} %slice.86) | copy-start | bytes 3133444
  129.8 1.2 copy-start.16
  130.7 3.1 copy-start.2
  132.1 0.8 copy-start.21
  132.2 1.6 copy-start.15
  133.0 0.8 copy-start.12
  138.4 2.9 copy-start
  138.4 3.4 copy-start.17
  138.5 5.0 copy-start.22
  148.0 1.0 copy-start.13
  149.9 1.3 copy-start.7
  150.1 2.1 copy-start.10
  230.4 182.7 %reduce-scatter.2.cloned.1.call-start = ((), (), s32[]{:S(2)}) async-start(), calls=%async_computation.2 | async-start | bytes 8912896 | tf_op jit(solution)/shard_map/reduce_scatter | solution.py:107
  238.2 1.4 copy-start.11
  238.2 277.3 %all-reduce.5.cloned.1.call-start = ((), (), s32[]{:S(2)}) async-start(), calls=%async_computation.4 | async-start | bytes 1605632 | tf_op jit(solution)/shard_map/psum | solution.py:138
  239.6 1.6 copy-start.3
  242.0 1.4 copy-start.8
  243.4 181.1 %collective-permute-start.3 = (f32[4,512]{1,0:T(4,128)S(1)}, f32[4,512]{1,0:T(4,128)S(1)}, u32[]{:S(2)}, u32[]{:S(2)}) collective-permute-start(f32[4,512]{1,0:T(4,128)S(1)} %slice.92), channel_id=1, source_target_pairs={{0,16},{16,32},{32,48},{48,64},{64,80},{80,96},{96,112},{112,128},... | collective-permute-start | bytes 24584 | tf_op jit(solution)/shard_map/ppermute | solution.py:19
  252.9 162.4 %copy-start.1 = (f32[32,8,4,512]{3,1,2,0:T(8,128)S(1)}, f32[32,8,4,512]{3,1,2,0:T(8,128)}, u32[]{:S(2)}) copy-start(f32[32,8,4,512]{3,1,2,0:T(8,128)} %copy.32) | copy-start | bytes 6291460
  419.6 3.0 copy-start.9
  422.6 1.9 copy-start.6
  517.2 1.8 copy-start.18
Sparse Core Ops, SparseCore 0:
  13.4 50.0 all-gather.1
  230.6 111.5 all-reduce.2
  344.9 68.2 reduce-scatter.1
  417.3 98.1 all-reduce.4
where the time goes:
time: 529 us; the launch traced here: 527 us
  waiting for transfers between devices  247 us (47%)
  local copies, waits for them, and re-layouts  161 us (30%)
  other arithmetic  59.2 us (11%)
  matrix products  34.6 us (7%)
  between operations  15.6 us (3%)
  starting transfers between devices  9.79 us (2%)
    psum x1, waiting for transfers between devices, per_device(): small = lax.psum(small, 'fsdp')  89.3 us
    psum x1, waiting for transfers between devices, per_device(): joined = lax.psum(jnp.concatenate([panel_part, small], 0), 'seq')  86.9 us
    reduce_scatter x1, waiting for transfers between devices, per_device(): lax.psum_scatter(proj_part, 'fsdp', scatter_dimension=0, tiled=True)  71 us
    reshape x2, local copies, waits for them, and re-layouts, window_grad(): blocks = full.reshape(STRIDE, GROUPS, CG, GROUPS, CG)  39.7 us
    dot_general x16, matrix products, dot_f32(): lax.dot_general(lhs, rhs, (dims, ((), ())), preferred_element_type=jnp.fl...  34.6 us
    reshape x1, local copies, waits for them, and re-layouts, per_device(): weight_lo = dense_weight[:STRIDE].reshape(half, row_width)  28.7 us
    reshape x1, local copies, waits for them, and re-layouts, per_device(): weight_hi = dense_weight[STRIDE:].reshape(half, row_width)  28.2 us
    slice x1, local copies, waits for them, and re-layouts, per_device(): weight_hi = dense_weight[STRIDE:].reshape(half, row_width)  25.7 us
  transfers between devices with their start and end apart: 8, of which 3 were waited for; matrix products, arithmetic and copies ran while one was open for 28% of the time, Pallas kernels for 0%

commit v1 on v0

--- a/solution.py
+++ b/solution.py
@@ -134,7 +134,8 @@
     grad_bytes = (upstream.astype(jnp.float32) + back_rows)[None]
     conv_size = conv_part.size
     small = jnp.concatenate([conv_part.reshape(-1), gain_part]).reshape(-1, row_width)
-    small = lax.psum(small, "fsdp")
+    terms = lax.all_gather(small, "fsdp")
+    small = jnp.sum(terms, axis=0)
     joined = lax.psum(jnp.concatenate([panel_part, small], 0), "seq")
     proj_sum = joined[:panel_rows]
     small_sum = joined[panel_rows:].reshape(-1)

time: 529 us -> 462 us (0.87)
  waiting for transfers between devices: 247 us -> 182 us
    psum x1 -> x0, waiting for transfers between devices: 89.3 us -> none  [per_device(): small = lax.psum(small, 'fsdp')]
    all_gather x0 -> x1, waiting for transfers between devices: none -> 29.1 us  [per_device(): terms = lax.all_gather(small, 'fsdp')]
    unnamed x54 -> x66, local copies, waits for them, and re-layouts: 13.2 us -> 12.8 us
  transfers between devices with their start and end apart: 8 -> 8, of which waited for: 3 -> 3; matrix products, arithmetic and copies ran while one was open for 28% -> 33% of each run, Pallas kernels for 0% -> 0%
where the time goes in v1:
time: 462 us; the launch traced here: 461 us
  waiting for transfers between devices  182 us (39%)
  local copies, waits for them, and re-layouts  162 us (35%)
  other arithmetic  60.1 us (13%)
  matrix products  31.3 us (7%)
  between operations  15.7 us (3%)
  starting transfers between devices  9.83 us (2%)
    psum x1, waiting for transfers between devices, per_device(): joined = lax.psum(jnp.concatenate([panel_part, small], 0), 'seq')  86.7 us
    reduce_scatter x1, waiting for transfers between devices, per_device(): lax.psum_scatter(proj_part, 'fsdp', scatter_dimension=0, tiled=True)  65.7 us
    reshape x2, local copies, waits for them, and re-layouts, window_grad(): blocks = full.reshape(STRIDE, GROUPS, CG, GROUPS, CG)  39.6 us
    dot_general x16, matrix products, dot_f32(): lax.dot_general(lhs, rhs, (dims, ((), ())), preferred_element_type=jnp.fl...  31.3 us
    all_gather x1, waiting for transfers between devices, per_device(): terms = lax.all_gather(small, 'fsdp')  29.1 us
    reshape x1, local copies, waits for them, and re-layouts, per_device(): weight_lo = dense_weight[:STRIDE].reshape(half, row_width)  28.7 us
    reshape x1, local copies, waits for them, and re-layouts, per_device(): weight_hi = dense_weight[STRIDE:].reshape(half, row_width)  28.2 us
    slice x1, local copies, waits for them, and re-layouts, per_device(): weight_hi = dense_weight[STRIDE:].reshape(half, row_width)  25.8 us
  transfers between devices with their start and end apart: 8, of which 3 were waited for; matrix products, arithmetic and copies ran while one was open for 33% of the time, Pallas kernels for 0%

profile of v1, /device:TPU:32, one launch (start us, length us, event | category | flops | bytes accessed | tf_op | source)
XLA Modules:
  0.0 460.7 jit_solution(11023715925383192615)
XLA Ops:
  8.0 1.3 collective-permute-start.1
  10.0 1.3 collective-permute-start
  11.9 1.3 collective-permute-start.2
  13.8 1.3 reduce.13
  16.3 1.5 slice.78
  17.8 1.2 slice.86
  19.0 1.6 reshape.259
  20.6 1.5 reshape_squeeze.11
  22.1 1.5 concatenate.56
  23.6 1.6 slice.94
  25.9 1.5 mul.283
  28.2 11.2 %broadcast_multiply_fusion = bf16[8,32,16,32,16]{4,3,2,1,0:T(8,128)(2,1)} fusion(bf16[32,32]{1,0:T(8,128)(2,1)S(1)} %fusion.39, bf16[8,32,16,16]{3,2,1,0:T(8,128)(2,1)S(1)} %copy.23), kind=kLoop, calls=%fused_computation.2 | loop fusion | flops 2097152 | bytes 4327424 | tf_op jit(solution)/shard_map/mul | solution.py:89
  39.4 25.8 %fusion.44 = (bf16[4,32,16,32,16]{4,3,2,1,0:T(8,128)(2,1)}, bf16[4,32,16,32,16]{4,3,2,1,0:T(8,128)(2,1)}) fusion(bf16[8,32,16,32,16]{4,3,2,1,0:T(8,128)(2,1)} %broadcast_multiply_fusion), kind=kLoop, calls=%fused_computation.87 | loop fusion | bytes 8388608 | tf_op jit(solution)/shard_map/slice | solution.py:93
  65.2 28.7 %reshape.249 = bf16[2048,512]{1,0:T(8,128)(2,1)} reshape(bf16[4,32,16,32,16]{4,3,2,1,0:T(8,128)(2,1)} %get-tuple-element.29) | data formatting | bytes 4194304 | tf_op jit(solution)/shard_map/reshape | solution.py:92
  93.9 28.2 %reshape.250 = bf16[2048,512]{1,0:T(8,128)(2,1)S(1)} reshape(bf16[4,32,16,32,16]{4,3,2,1,0:T(8,128)(2,1)} %get-tuple-element.28) | data formatting | bytes 4194304 | tf_op jit(solution)/shard_map/reshape | solution.py:93
  122.1 1.6 slice.87
  123.7 2.6 fusion.45
  127.0 2.2 copy.32
  134.2 4.5 fusion.15
  141.3 1.8 fusion.8
  144.4 1.1 copy-done.7
  146.3 2.8 convolution_add_fusion.1
  149.1 19.8 %reshape.255 = f32[4,32,16,32,16]{4,3,2,1,0:T(8,128)} reshape(f32[2048,512]{1,0:T(8,128)} %convolution_add_fusion.1) | data formatting | bytes 8388608 | tf_op jit(solution)/shard_map/reshape | solution.py:120
  168.9 1.7 fusion.50
  170.6 2.8 convolution_add_fusion
  173.4 19.8 %reshape.257 = f32[4,32,16,32,16]{4,3,2,1,0:T(8,128)} reshape(f32[2048,512]{1,0:T(8,128)} %convolution_add_fusion) | data formatting | bytes 8388608 | tf_op jit(solution)/shard_map/reshape | solution.py:120
  193.2 25.6 %multiply_reduce_fusion.1 = (f32[4,32,16,16]{3,2,1,0:T(8,128)S(1)}, f32[4,32,16,16]{3,2,1,0:T(8,128)}) fusion(f32[4,32,16,32,16]{4,3,2,1,0:T(8,128)} %reshape.255, f32[32,32]{1,0:T(8,128)S(1)} %fusion.38, f32[4,32,16,32,16]{4,3,2,1,0:T(8,128)} %reshape.257), kind=kLoop, calls=%fused_computation.1 | loop fusion | flops 4128768 | bytes 8654848 | tf_op jit(solution)/shard_map/reduce_sum | solution.py:122
  218.8 2.7 pad_maximum_fusion.1
  221.5 2.9 reshape.258
  224.4 1.7 pad_maximum_fusion.3
  226.1 1.7 all_gather_reshape.3
  227.9 1.8 fusion.49
  230.4 4.2 pad_maximum_fusion
  238.5 1.3 copy-done.8
  239.8 5.8 %collective-permute-start.3 = (f32[4,512]{1,0:T(4,128)S(1)}, f32[4,512]{1,0:T(4,128)S(1)}, u32[]{:S(2)}, u32[]{:S(2)}) collective-permute-start(f32[4,512]{1,0:T(4,128)S(1)} %slice.92), channel_id=1, source_target_pairs={{0,16},{16,32},{32,48},{48,64},{64,80},{80,96},{96,112},{112,128},... | collective-permute-start | bytes 24584 | tf_op jit(solution)/shard_map/ppermute | solution.py:19
  245.6 3.7 fusion.46
  249.3 29.1 %all-gather.5.cloned.1.call-done = f32[16,129,512]{2,1,0:T(8,128)} async-done(((f32[1,129,512]{2,1,0:T(8,128)}), f32[16,129,512]{2,1,0:T(8,128)}) %all-gather.5.cloned.1.call-update) | async-done | bytes 4227088 | tf_op jit(solution)/shard_map/all_gather | solution.py:137
  278.3 2.8 reduce_sum.59
  281.1 65.7 %reduce-scatter.2.cloned.1.call-done = f32[256,512]{1,0:T(8,128)} async-done(((f32[4096,512]{1,0:T(8,128)}), f32[256,512]{1,0:T(8,128)}) %reduce-scatter.2.cloned.1.call-update) | async-done | bytes 524304 | tf_op jit(solution)/shard_map/reduce_scatter | solution.py:107
  346.8 2.0 pad_maximum_fusion.2
  348.9 4.3 fusion.1
  353.1 3.0 reshape.254
  356.2 1.9 concatenate.64
  358.1 4.1 fusion.16
  362.2 86.7 %all-reduce.2.cloned.1.call-done = f32[385,512]{1,0:T(8,128)} async-done(((f32[385,512]{1,0:T(8,128)}), f32[385,512]{1,0:T(8,128)}) %all-reduce.2.cloned.1.call-update) | async-done | bytes 788496 | tf_op jit(solution)/shard_map/psum | solution.py:139
  448.9 1.0 slice_multiply_fusion.1
  450.6 1.8 copy.30
  453.0 1.2 fusion.37
  (116 shorter events, 20.0 us)
Async XLA Ops:
  7.2 10.6 %copy-start.5 = (bf16[1,1024,512]{2,1,0:T(8,128)(2,1)S(1)}, bf16[1,1024,512]{2,1,0:T(8,128)(2,1)}, u32[]{:S(2)}) copy-start(bf16[1,1024,512]{2,1,0:T(8,128)(2,1)} %param.9) | copy-start | bytes 3145732
  7.2 127.0 %all-gather.3.cloned.1.call-start = ((), (), s32[]{:S(2)}) async-start(), calls=%async_computation.1 | async-start | bytes 4456448 | tf_op jit(solution)/shard_map/all_gather | solution.py:97
  8.0 118.4 %collective-permute-start.1 = (s32[4]{0:T(128)S(1)}, s32[4]{0:T(128)S(1)}, u32[]{:S(2)}, u32[]{:S(2)}) collective-permute-start(s32[4]{0:T(128)S(1)} %slice_bitcast_fusion.2), channel_id=1, source_target_pairs={{16,0},{32,16},{48,32},{64,48},{80,64},{96,80},{112,96},{128,112},... | collective-permute-start | bytes 56 | tf_op jit(solution)/shard_map/ppermute | solution.py:19
  10.0 120.8 %collective-permute-start = (bf16[4,512]{1,0:T(4,128)(2,1)S(1)}, bf16[4,512]{1,0:T(4,128)(2,1)S(1)}, u32[]{:S(2)}, u32[]{:S(2)}) collective-permute-start(bf16[4,512]{1,0:T(4,128)(2,1)S(1)} %slice_bitcast_fusion.1), channel_id=1, source_target_pairs={{16,0},{32,16},{48,32},{64,48},{80,64},{96,80},{112,96},{128,112},... | collective-permute-start | bytes 12296 | tf_op jit(solution)/shard_map/ppermute | solution.py:19
  11.9 120.2 %collective-permute-start.2 = (bf16[4,512]{1,0:T(4,128)(2,1)S(1)}, bf16[4,512]{1,0:T(4,128)(2,1)S(1)}, u32[]{:S(2)}, u32[]{:S(2)}) collective-permute-start(bf16[4,512]{1,0:T(4,128)(2,1)S(1)} %slice_bitcast_fusion), channel_id=1, source_target_pairs={{16,0},{32,16},{48,32},{64,48},{80,64},{96,80},{112,96},{128,112},... | collective-permute-start | bytes 12296 | tf_op jit(solution)/shard_map/ppermute | solution.py:19
  13.3 265.1 %all-gather.5.cloned.1.call-start = ((), (), s32[]{:S(2)}) async-start(), calls=%async_computation.3 | async-start | bytes 4734976 | tf_op jit(solution)/shard_map/all_gather | solution.py:137
  17.8 2.8 copy-start.4
  22.1 3.6 copy-start.26
  25.7 1.7 copy-start.25
  93.9 28.2 %copy-start.14 = (bf16[1,1020,512]{2,1,0:T(8,128)(2,1)S(1)}, bf16[1,1020,512]{2,1,0:T(8,128)(2,1)}, u32[]{:S(2)}) copy-start(bf16[1,1020,512]{2,1,0:T(8,128)(2,1)} %slice.86) | copy-start | bytes 3133444
  129.9 1.2 copy-start.16
  130.8 3.1 copy-start.2
  132.2 0.8 copy-start.27
  132.2 1.6 copy-start.15
  133.0 0.8 copy-start.12
  133.2 6.5 %copy-start.21 = (bf16[256,512]{1,0:T(8,128)(2,1)}, bf16[256,512]{1,0:T(8,128)(2,1)S(1)}, u32[]{:S(2)}) copy-start(bf16[256,512]{1,0:T(8,128)(2,1)S(1)} %multiply_convert_fusion) | copy-start | bytes 786436
  134.2 4.5 copy-start.28
  138.7 1.0 copy-start.17
  138.7 2.0 copy-start
  138.7 2.6 copy-start.23
  141.3 1.8 copy-start.13
  143.1 1.0 copy-start.19
  144.2 1.3 copy-start.7
  144.4 1.9 copy-start.10
  221.5 6.3 %copy-start.18 = (bf16[256,2048]{1,0:T(8,128)(2,1)S(1)}, bf16[256,2048]{1,0:T(8,128)(2,1)}, u32[]{:S(2)}) copy-start(bf16[256,2048]{1,0:T(8,128)(2,1)} %copy-done.17) | copy-start | bytes 3145732
  227.8 119.1 %reduce-scatter.2.cloned.1.call-start = ((), (), s32[]{:S(2)}) async-start(), calls=%async_computation.2 | async-start | bytes 8912896 | tf_op jit(solution)/shard_map/reduce_scatter | solution.py:107
  227.8 1.8 copy-start.20
  227.8 1.8 copy-start.22
  234.6 1.4 copy-start.11
  234.6 214.2 %all-reduce.2.cloned.1.call-start = ((), (), s32[]{:S(2)}) async-start(), calls=%async_computation.4 | async-start | bytes 1605632 | tf_op jit(solution)/shard_map/psum | solution.py:139
  236.0 1.6 copy-start.3
  238.4 1.3 copy-start.8
  239.8 118.3 %collective-permute-start.3 = (f32[4,512]{1,0:T(4,128)S(1)}, f32[4,512]{1,0:T(4,128)S(1)}, u32[]{:S(2)}, u32[]{:S(2)}) collective-permute-start(f32[4,512]{1,0:T(4,128)S(1)} %slice.92), channel_id=1, source_target_pairs={{0,16},{16,32},{32,48},{48,64},{64,80},{80,96},{96,112},{112,128},... | collective-permute-start | bytes 24584 | tf_op jit(solution)/shard_map/ppermute | solution.py:19
  281.1 67.7 %copy-start.1 = (f32[32,8,4,512]{3,1,2,0:T(8,128)S(1)}, f32[32,8,4,512]{3,1,2,0:T(8,128)}, u32[]{:S(2)}) copy-start(f32[32,8,4,512]{3,1,2,0:T(8,128)} %copy.32) | copy-start | bytes 6291460
  353.1 3.0 copy-start.9
  356.2 1.9 copy-start.6
  450.6 1.8 copy-start.24
Sparse Core Ops, SparseCore 0:
  13.4 50.0 all-gather.2
  227.9 50.4 all-gather.4
  280.9 65.9 reduce-scatter.1
  350.6 98.2 all-reduce.1
